TPU v7x, 32 devices: a whole 2x2x4 slice. The times are simulated.
32 devices in a mesh: shift: 4 (over y, x), rows: 8 (over z, core).
Axes of the slice: x: 2, y: 2, z: 4, core: 2. Of those that a mesh axis runs over, the one named last changes fastest.
Arguments:
- filtered: bfloat16 [4, 131072, 256], P('shift', 'rows'), as said below
- weights: float32 [4, 256], P('shift'), may hold values from 0.25 to 2
Outputs:
- basis: float32 [131072, 256], P(('rows', 'shift'))
- r_factor: float32 [256, 256], replicated
Inputs may be any that keep to these rules, and one draw needn't show every extreme that they name: Each filtered block is of full rank.
All inputs are finite; a program needn't handle non-finite values.
Results may differ from a plain program's by a relative error of at most 0.0003.
Values sent between devices are 32-bit elements; how exact they have to be, the bound alone decides.
No kernel may reach another device: no remote copies, remote signals or barrier semaphores. Data moves between devices by JAX's collectives and lax.ppermute only.
A program may use at most 128 MiB of HBM per device.

v0:
```python
import jax
import jax.numpy as jnp
from jax import lax
from jax.sharding import PartitionSpec as P


def cross_products(left, right):
    return jnp.dot(
        left.T, right, precision=lax.Precision.HIGHEST, preferred_element_type=jnp.float32
    )


def shards(filtered, weights):
    weighted = filtered[0].astype(jnp.float32) * weights[0][None, :]
    mixed = lax.psum_scatter(weighted, "shift", scatter_dimension=0, tiled=True)
    devices_all = lax.axis_size(("shift", "rows"))
    total_rows = mixed.shape[0] * devices_all
    gram = cross_products(mixed, mixed) / total_rows
    lower = jnp.linalg.cholesky(lax.psum(gram, ("shift", "rows")))
    basis = jax.scipy.linalg.solve_triangular(lower, mixed.T, lower=True).T
    return (basis, lower.T)


def solution(mesh):
    in_specs = (P("shift", "rows", None), P("shift", None))
    out_specs = (P(("rows", "shift"), None), P())
    return jax.shard_map(shards, mesh=mesh, in_specs=in_specs, out_specs=out_specs, check_vma=False)
```

profile of v0, /device:TPU:0, one launch (start us, length us, event | category | flops | bytes accessed | tf_op | source)
XLA Modules:
  0.0 396.4 jit_solution(7916319687444031821)
XLA Ops:
  7.2 0.0 reduce-scatter.2.cloned.1.call-start
  7.2 9.6 %convert_multiply_fusion = f32[16384,256]{1,0:T(8,128)} fusion(bf16[1,16384,256]{2,1,0:T(8,128)(2,1)} %param.2, f32[256]{0:T(256)} %bitcast.44), kind=kLoop, calls=%fused_computation.2 | loop fusion | flops 8388608 | bytes 25166848 | tf_op jit(solution)/shard_map/mul | solution.py:14
  16.8 0.0 reduce-scatter.2.cloned.1.call-update
  16.8 0.0 all-reduce.3.cloned.1.call-start
  16.9 156.7 %reduce-scatter.2.cloned.1.call-done = f32[4096,256]{1,0:T(8,128)} async-done(((f32[16384,256]{1,0:T(8,128)}), f32[4096,256]{1,0:T(8,128)}) %reduce-scatter.2.cloned.1.call-update) | async-done | bytes 4194320 | tf_op jit(solution)/shard_map/reduce_scatter | solution.py:15
  173.5 10.9 %convolution_multiply_fusion = f32[256,256]{0,1:T(8,128)} fusion(f32[4096,256]{1,0:T(8,128)} %reduce-scatter.2.cloned.1.call-done), kind=kOutput, calls=%fused_computation.7 | convolution fusion | flops 3221291008 | bytes 4456448 | tf_op jit(solution)/shard_map/dot_general | solution.py:8
  184.4 0.0 all-reduce.3.cloned.1.call-update
  184.5 125.1 %all-reduce.3.cloned.1.call-done = f32[256,256]{0,1:T(8,128)} async-done(((f32[256,256]{0,1:T(8,128)}), f32[256,256]{0,1:T(8,128)}) %all-reduce.3.cloned.1.call-update) | async-done | bytes 262160 | tf_op jit(solution)/shard_map/psum | solution.py:19
  309.6 1.1 copy.5
  310.7 1.0 fusion.2
  311.7 11.7 %cholesky.50 = f32[128,128]{1,0:T(8,128)S(1)} custom-call(f32[128,128]{1,0:T(8,128)S(1)} %cholesky.118), custom_call_target="Cholesky" | custom-call | tf_op jit(solution)/shard_map/jit(cholesky)/cholesky | solution.py:19
  323.4 10.0 %custom-call.15 = f32[1,128,128]{1,2,0:T(8,128)S(1)} custom-call(f32[1,128,128]{2,1,0:T(8,128)S(1)} %get-tuple-element.27), custom_call_target="InvertDiagBlocksLowerTriangular" | custom-call | tf_op jit(solution)/shard_map/jit(cholesky)/cholesky | solution.py:19
  333.4 0.2 constant_dynamic-update-slice_fusion.1
  333.7 0.3 convolution_subtract_fusion.1
  333.9 11.7 %cholesky.105 = f32[128,128]{1,0:T(8,128)S(1)} custom-call(f32[128,128]{1,0:T(8,128)S(1)} %convolution_subtract_fusion.1), custom_call_target="Cholesky" | custom-call | tf_op jit(solution)/shard_map/jit(cholesky)/cholesky | solution.py:19
  345.7 0.7 compare_reduce_fusion
  347.8 0.1 triangular_solve.57
  347.9 4.1 %while.1 = (s32[]{:T(128)}, f32[256,256]{1,0:T(8,128)S(1)}, s32[2,2]{1,0:T(2,128)S(1)}, f32[2,128,128]{2,1,0:T(8,128)S(1)}, s32[]{:T(128)}) while((s32[]{:T(128)}, f32[256,256]{1,0:T(8,128)S(1)}, s32[2,2]{1,0:T(2,128)S(1)}, f32[2,128,128]{2,1,0:T(8,128)S(1)}, s32[]{:T(128)}) %tuple.29), condition=%wide.while_cond, body=%wide.while_body.sunk | while | flops 2 | bytes 131181 | solution.py:20
  347.9 0.6 fusion.18
  348.5 1.4 bitcast_dynamic-update-slice_fusion.2
  349.9 0.6 fusion.18
  350.5 1.4 bitcast_dynamic-update-slice_fusion.2
  352.0 19.7 %custom-call.16 = f32[2,128,128]{1,2,0:T(8,128)S(1)} custom-call(f32[2,128,128]{2,1,0:T(8,128)S(1)} %get-tuple-element.9), custom_call_target="InvertDiagBlocksLowerTriangular" | custom-call | tf_op jit(solution)/shard_map/jit(_solve_triangular)/triangular_solve | solution.py:20
  371.6 0.0 copy-start
  371.6 3.7 fusion
  375.3 0.0 copy-done
  375.3 3.4 convolution_subtract_fusion
  378.8 2.0 fusion.6
  380.8 2.4 maximum_bitcast_fusion
  383.2 5.6 %copy.6 = f32[4096,256]{1,0:T(8,128)} copy(f32[4096,256]{0,1:T(8,128)} %maximum_bitcast_fusion) | data formatting | bytes 8388608
  388.8 0.8 copy.7
  (9 shorter events, 0.2 us)
Async XLA Ops:
  7.2 166.4 %reduce-scatter.2.cloned.1.call-start = ((), (), s32[]{:S(2)}) async-start(), calls=%async_computation.1 | async-start | bytes 20971520 | tf_op jit(solution)/shard_map/reduce_scatter | solution.py:15
  16.8 292.8 %all-reduce.3.cloned.1.call-start = ((), (), s32[]{:S(2)}) async-start(), calls=%async_computation.2 | async-start | bytes 524288 | tf_op jit(solution)/shard_map/psum | solution.py:19
  371.6 3.7 copy-start
Sparse Core Ops, SparseCore 0:
  17.0 156.5 reduce-scatter.1
  184.6 124.9 all-reduce.2
where the time goes:
time: 397 us; the launch traced here: 396 us
  waiting for transfers between devices  282 us (71%)
  other arithmetic  66.9 us (17%)
  matrix products  20.5 us (5%)
  between operations  15.5 us (4%)
  local copies, waits for them, and re-layouts  11.7 us (3%)
    reduce_scatter x1, waiting for transfers between devices, shards(): mixed = lax.psum_scatter(weighted, 'shift', scatter_dimension=0, tiled=True)  157 us
    psum x1, waiting for transfers between devices, shards(): lower = jnp.linalg.cholesky(lax.psum(gram, ('shift', 'rows')))  125 us
    another operation x6, other arithmetic, shards(): lower = jnp.linalg.cholesky(lax.psum(gram, ('shift', 'rows')))  34.2 us
    another operation x2, other arithmetic, shards(): basis = jax.scipy.linalg.solve_triangular(lower, mixed.T, lower=True).T  19.7 us
    dot_general x1, matrix products, cross_products(): jnp.dot(left.T, right, precision=lax.Precision.HIGHEST, preferred_element...  10.9 us
    mul x1, other arithmetic, shards(): weighted = filtered[0].astype(jnp.float32) * weights[0][None, :]  9.6 us
    another operation x3, matrix products, shards(): basis = jax.scipy.linalg.solve_triangular(lower, mixed.T, lower=True).T  9.09 us
  transfers between devices with their start and end apart: 2, of which 2 were waited for; matrix products, arithmetic and copies ran while one was open for 0% of the time, Pallas kernels for 0%

commit v1 on v0

--- a/solution.py
+++ b/solution.py
@@ -16,7 +16,7 @@
     devices_all = lax.axis_size(("shift", "rows"))
     total_rows = mixed.shape[0] * devices_all
     gram = cross_products(mixed, mixed) / total_rows
-    lower = jnp.linalg.cholesky(lax.psum(gram, ("shift", "rows")))
+    lower = jnp.linalg.cholesky(lax.psum(lax.psum(gram, "rows"), "shift"))
     basis = jax.scipy.linalg.solve_triangular(lower, mixed.T, lower=True).T
     return (basis, lower.T)
 

time: 397 us -> 372 us (0.937)
  waiting for transfers between devices: 282 us -> 257 us
    psum x1 -> x2, waiting for transfers between devices: 125 us -> 99.9 us  [shards(): lower = jnp.linalg.cholesky(lax.psum(lax.psum(gram, 'rows'), 'shift'))]
  transfers between devices with their start and end apart: 2 -> 3, of which waited for: 2 -> 3; matrix products, arithmetic and copies ran while one was open for 0% -> 0% of each run, Pallas kernels for 0% -> 0%
where the time goes in v1:
time: 372 us; the launch traced here: 371 us
  waiting for transfers between devices  257 us (69%)
  other arithmetic  66.7 us (18%)
  matrix products  20.5 us (6%)
  between operations  15.2 us (4%)
  local copies, waits for them, and re-layouts  11.7 us (3%)
    reduce_scatter x1, waiting for transfers between devices, shards(): mixed = lax.psum_scatter(weighted, 'shift', scatter_dimension=0, tiled=True)  157 us
    psum x2, waiting for transfers between devices, shards(): lower = jnp.linalg.cholesky(lax.psum(lax.psum(gram, 'rows'), 'shift'))  99.9 us
    another operation x6, other arithmetic, shards(): lower = jnp.linalg.cholesky(lax.psum(lax.psum(gram, 'rows'), 'shift'))  34 us
    another operation x2, other arithmetic, shards(): basis = jax.scipy.linalg.solve_triangular(lower, mixed.T, lower=True).T  19.7 us
    dot_general x1, matrix products, cross_products(): jnp.dot(left.T, right, precision=lax.Precision.HIGHEST, preferred_element...  10.9 us
    mul x1, other arithmetic, shards(): weighted = filtered[0].astype(jnp.float32) * weights[0][None, :]  9.6 us
    another operation x3, matrix products, shards(): basis = jax.scipy.linalg.solve_triangular(lower, mixed.T, lower=True).T  9.09 us
  transfers between devices with their start and end apart: 3, of which 3 were waited for; matrix products, arithmetic and copies ran while one was open for 0% of the time, Pallas kernels for 0%

profile of v1, /device:TPU:0, one launch (start us, length us, event | category | flops | bytes accessed | tf_op | source)
XLA Modules:
  0.0 371.2 jit_solution(14428343768684158041)
XLA Ops:
  7.2 0.0 reduce-scatter.2.cloned.1.call-start
  7.2 9.6 %convert_multiply_fusion = f32[16384,256]{1,0:T(8,128)} fusion(bf16[1,16384,256]{2,1,0:T(8,128)(2,1)} %param.2, f32[256]{0:T(256)} %bitcast.44), kind=kLoop, calls=%fused_computation.2 | loop fusion | flops 8388608 | bytes 25166848 | tf_op jit(solution)/shard_map/mul | solution.py:14
  16.8 0.0 reduce-scatter.2.cloned.1.call-update
  16.8 0.0 all-reduce.4.cloned.1.call-start
  16.9 156.7 %reduce-scatter.2.cloned.1.call-done = f32[4096,256]{1,0:T(8,128)} async-done(((f32[16384,256]{1,0:T(8,128)}), f32[4096,256]{1,0:T(8,128)}) %reduce-scatter.2.cloned.1.call-update) | async-done | bytes 4194320 | tf_op jit(solution)/shard_map/reduce_scatter | solution.py:15
  173.5 10.9 %convolution_multiply_fusion = f32[256,256]{0,1:T(8,128)} fusion(f32[4096,256]{1,0:T(8,128)} %reduce-scatter.2.cloned.1.call-done), kind=kOutput, calls=%fused_computation.7 | convolution fusion | flops 3221291008 | bytes 4456448 | tf_op jit(solution)/shard_map/dot_general | solution.py:8
  184.4 0.0 all-reduce.4.cloned.1.call-update
  184.5 0.2 all-reduce.6.cloned.1.call-start
  184.7 54.8 %all-reduce.4.cloned.1.call-done = f32[256,256]{0,1:T(8,128)} async-done(((f32[256,256]{0,1:T(8,128)}), f32[256,256]{0,1:T(8,128)}) %all-reduce.4.cloned.1.call-update) | async-done | bytes 262160 | tf_op jit(solution)/shard_map/psum | solution.py:19
  239.5 0.0 all-reduce.6.cloned.1.call-update
  239.6 45.1 %all-reduce.6.cloned.1.call-done = f32[256,256]{0,1:T(8,128)} async-done(((f32[256,256]{0,1:T(8,128)}), f32[256,256]{0,1:T(8,128)}) %all-reduce.6.cloned.1.call-update) | async-done | bytes 262160 | tf_op jit(solution)/shard_map/psum | solution.py:19
  284.6 1.1 copy.5
  285.7 1.0 fusion.2
  286.7 11.7 %cholesky.50 = f32[128,128]{1,0:T(8,128)S(1)} custom-call(f32[128,128]{1,0:T(8,128)S(1)} %cholesky.118), custom_call_target="Cholesky" | custom-call | tf_op jit(solution)/shard_map/jit(cholesky)/cholesky | solution.py:19
  298.5 9.8 %custom-call.15 = f32[1,128,128]{1,2,0:T(8,128)S(1)} custom-call(f32[1,128,128]{2,1,0:T(8,128)S(1)} %get-tuple-element.27), custom_call_target="InvertDiagBlocksLowerTriangular" | custom-call | tf_op jit(solution)/shard_map/jit(cholesky)/cholesky | solution.py:19
  308.3 0.2 constant_dynamic-update-slice_fusion.1
  308.5 0.3 convolution_subtract_fusion.1
  308.8 11.7 %cholesky.105 = f32[128,128]{1,0:T(8,128)S(1)} custom-call(f32[128,128]{1,0:T(8,128)S(1)} %convolution_subtract_fusion.1), custom_call_target="Cholesky" | custom-call | tf_op jit(solution)/shard_map/jit(cholesky)/cholesky | solution.py:19
  320.5 0.7 compare_reduce_fusion
  322.7 0.1 triangular_solve.57
  322.7 4.3 %while.1 = (s32[]{:T(128)}, f32[256,256]{1,0:T(8,128)S(1)}, s32[2,2]{1,0:T(2,128)S(1)}, f32[2,128,128]{2,1,0:T(8,128)S(1)}, s32[]{:T(128)}) while((s32[]{:T(128)}, f32[256,256]{1,0:T(8,128)S(1)}, s32[2,2]{1,0:T(2,128)S(1)}, f32[2,128,128]{2,1,0:T(8,128)S(1)}, s32[]{:T(128)}) %tuple.29), condition=%wide.while_cond, body=%wide.while_body.sunk | while | flops 2 | bytes 131181 | solution.py:20
  322.9 0.6 fusion.18
  323.5 1.4 bitcast_dynamic-update-slice_fusion.2
  325.0 0.6 fusion.18
  325.6 1.4 bitcast_dynamic-update-slice_fusion.2
  327.0 19.7 %custom-call.16 = f32[2,128,128]{1,2,0:T(8,128)S(1)} custom-call(f32[2,128,128]{2,1,0:T(8,128)S(1)} %get-tuple-element.9), custom_call_target="InvertDiagBlocksLowerTriangular" | custom-call | tf_op jit(solution)/shard_map/jit(_solve_triangular)/triangular_solve | solution.py:20
  346.7 0.0 copy-start
  346.7 3.7 fusion
  350.4 0.0 copy-done
  350.4 3.4 convolution_subtract_fusion
  353.8 2.0 fusion.6
  355.8 2.4 maximum_bitcast_fusion
  358.2 5.6 %copy.6 = f32[4096,256]{1,0:T(8,128)} copy(f32[4096,256]{0,1:T(8,128)} %maximum_bitcast_fusion) | data formatting | bytes 8388608
  363.8 0.8 copy.7
  (9 shorter events, 0.2 us)
Async XLA Ops:
  7.2 166.4 %reduce-scatter.2.cloned.1.call-start = ((), (), s32[]{:S(2)}) async-start(), calls=%async_computation.1 | async-start | bytes 20971520 | tf_op jit(solution)/shard_map/reduce_scatter | solution.py:15
  16.8 222.7 %all-reduce.4.cloned.1.call-start = ((), (), s32[]{:S(2)}) async-start(), calls=%async_computation.2 | async-start | bytes 524288 | tf_op jit(solution)/shard_map/psum | solution.py:19
  184.5 100.2 %all-reduce.6.cloned.1.call-start = ((), (), s32[]{:S(2)}) async-start(), calls=%async_computation.3 | async-start | bytes 524288 | tf_op jit(solution)/shard_map/psum | solution.py:19
  346.7 3.7 copy-start
Sparse Core Ops, SparseCore 0:
  17.0 156.5 reduce-scatter.1
  184.6 54.8 all-reduce.3
  242.7 41.8 all-reduce.5

commit v2 on v0

--- a/solution.py
+++ b/solution.py
@@ -16,7 +16,7 @@
     devices_all = lax.axis_size(("shift", "rows"))
     total_rows = mixed.shape[0] * devices_all
     gram = cross_products(mixed, mixed) / total_rows
-    lower = jnp.linalg.cholesky(lax.psum(gram, ("shift", "rows")))
+    lower = jnp.linalg.cholesky(jnp.sum(lax.all_gather(gram, ("shift", "rows")), axis=0))
     basis = jax.scipy.linalg.solve_triangular(lower, mixed.T, lower=True).T
     return (basis, lower.T)
 

time: 397 us -> 351 us (0.88)
  waiting for transfers between devices: 282 us -> 234 us
    psum x1 -> x0, waiting for transfers between devices: 125 us -> none  [shards(): lower = jnp.linalg.cholesky(lax.psum(gram, ('shift', 'rows')))]
    all_gather x0 -> x1, waiting for transfers between devices: none -> 77.5 us  [shards(): lax.all_gather(gram, ('shift', 'rows'))]
where the time goes in v2:
time: 351 us
  waiting for transfers between devices  234 us (67%)
  other arithmetic  69.8 us (20%)
  matrix products  20.5 us (6%)
  between operations  15.5 us (4%)
  local copies, waits for them, and re-layouts  10.7 us (3%)
    reduce_scatter x1, waiting for transfers between devices, shards(): mixed = lax.psum_scatter(weighted, 'shift', scatter_dimension=0, tiled=True)  157 us
    all_gather x1, waiting for transfers between devices, shards(): lax.all_gather(gram, ('shift', 'rows'))  77.5 us
    another operation x6, other arithmetic, shards(): jnp.linalg.cholesky(jnp.sum(lax.all_gather(gram, ('shift', 'rows')), axis...  34.2 us
    another operation x2, other arithmetic, shards(): basis = jax.scipy.linalg.solve_triangular(lower, mixed.T, lower=True).T  19.7 us
    dot_general x1, matrix products, cross_products(): jnp.dot(left.T, right, precision=lax.Precision.HIGHEST, preferred_element...  10.9 us
    mul x1, other arithmetic, shards(): weighted = filtered[0].astype(jnp.float32) * weights[0][None, :]  9.6 us
    another operation x3, matrix products, shards(): basis = jax.scipy.linalg.solve_triangular(lower, mixed.T, lower=True).T  9.09 us
  transfers between devices with their start and end apart: 2, of which 2 were waited for; matrix products, arithmetic and copies ran while one was open for 0% of the time, Pallas kernels for 0%

profile of v2, /device:TPU:0, one launch (start us, length us, event | category | flops | bytes accessed | tf_op | source)
XLA Modules:
  0.0 350.9 jit_solution(9389313986666459823)
XLA Ops:
  7.2 0.0 reduce-scatter.2.cloned.1.call-start
  7.2 9.6 %convert_multiply_fusion = f32[16384,256]{1,0:T(8,128)} fusion(bf16[1,16384,256]{2,1,0:T(8,128)(2,1)} %param.2, f32[256]{0:T(256)} %bitcast.46), kind=kLoop, calls=%fused_computation.2 | loop fusion | flops 8388608 | bytes 25166848 | tf_op jit(solution)/shard_map/mul | solution.py:14
  16.8 0.0 reduce-scatter.2.cloned.1.call-update
  16.8 0.0 all-gather.3.cloned.1.call-start
  16.9 156.7 %reduce-scatter.2.cloned.1.call-done = f32[4096,256]{1,0:T(8,128)} async-done(((f32[16384,256]{1,0:T(8,128)}), f32[4096,256]{1,0:T(8,128)}) %reduce-scatter.2.cloned.1.call-update) | async-done | bytes 4194320 | tf_op jit(solution)/shard_map/reduce_scatter | solution.py:15
  173.5 10.9 %convolution_multiply_fusion = f32[256,256]{1,0:T(8,128)} fusion(f32[4096,256]{1,0:T(8,128)} %reduce-scatter.2.cloned.1.call-done), kind=kOutput, calls=%fused_computation.7 | convolution fusion | flops 3221291008 | bytes 4456448 | tf_op jit(solution)/shard_map/dot_general | solution.py:8
  184.5 0.0 all-gather.3.cloned.1.call-update
  184.5 77.5 %all-gather.3.cloned.1.call-done = f32[8192,256]{1,0:T(8,128)} async-done(((f32[256,256]{1,0:T(8,128)}), f32[8192,256]{1,0:T(8,128)}) %all-gather.3.cloned.1.call-update) | async-done | bytes 8388624 | tf_op jit(solution)/shard_map/all_gather | solution.py:19
  262.0 3.9 %reduce_sum.9 = f32[256,256]{1,0:T(8,128)S(1)} reduce(f32[32,256,256]{2,1,0:T(8,128)} %bitcast.45, f32[]{:T(128)} %constant.78.clone.1), dimensions={0}, to_apply=%region_1.0 | reduce | flops 2031616 | bytes 8650756 | tf_op jit(solution)/shard_map/reduce_sum | solution.py:19
  266.0 0.1 copy.7
  266.1 11.7 %cholesky.50 = f32[128,128]{1,0:T(8,128)S(1)} custom-call(f32[128,128]{1,0:T(8,128)S(1)} %cholesky.118), custom_call_target="Cholesky" | custom-call | tf_op jit(solution)/shard_map/jit(cholesky)/cholesky | solution.py:19
  277.9 9.9 %custom-call.15 = f32[1,128,128]{1,2,0:T(8,128)S(1)} custom-call(f32[1,128,128]{2,1,0:T(8,128)S(1)} %get-tuple-element.29), custom_call_target="InvertDiagBlocksLowerTriangular" | custom-call | tf_op jit(solution)/shard_map/jit(cholesky)/cholesky | solution.py:19
  287.9 0.2 constant_dynamic-update-slice_fusion.1
  288.1 0.3 convolution_subtract_fusion.1
  288.3 11.7 %cholesky.105 = f32[128,128]{1,0:T(8,128)S(1)} custom-call(f32[128,128]{1,0:T(8,128)S(1)} %convolution_subtract_fusion.1), custom_call_target="Cholesky" | custom-call | tf_op jit(solution)/shard_map/jit(cholesky)/cholesky | solution.py:19
  300.1 0.7 compare_reduce_fusion
  302.2 0.1 triangular_solve.57
  302.3 4.1 %while.1 = (s32[]{:T(128)}, f32[256,256]{1,0:T(8,128)S(1)}, s32[2,2]{1,0:T(2,128)S(1)}, f32[2,128,128]{2,1,0:T(8,128)S(1)}, s32[]{:T(128)}) while((s32[]{:T(128)}, f32[256,256]{1,0:T(8,128)S(1)}, s32[2,2]{1,0:T(2,128)S(1)}, f32[2,128,128]{2,1,0:T(8,128)S(1)}, s32[]{:T(128)}) %tuple.30), condition=%wide.while_cond, body=%wide.while_body.sunk | while | flops 2 | bytes 131181 | solution.py:20
  302.3 0.6 fusion.18
  302.9 1.4 bitcast_dynamic-update-slice_fusion.2
  304.3 0.6 fusion.18
  304.9 1.4 bitcast_dynamic-update-slice_fusion.2
  306.4 19.7 %custom-call.16 = f32[2,128,128]{1,2,0:T(8,128)S(1)} custom-call(f32[2,128,128]{2,1,0:T(8,128)S(1)} %get-tuple-element.9), custom_call_target="InvertDiagBlocksLowerTriangular" | custom-call | tf_op jit(solution)/shard_map/jit(_solve_triangular)/triangular_solve | solution.py:20
  326.1 0.0 copy-start
  326.1 3.7 %fusion = f32[128,4096]{1,0:T(8,128)S(1)} fusion(f32[256,4096]{0,1:T(8,128)} %bitcast.43, f32[2,128,128]{1,2,0:T(8,128)S(1)} %custom-call.16), kind=kOutput, calls=%fused_computation.5 | convolution fusion | flops 805306368 | bytes 4259840 | tf_op jit(solution)/shard_map/jit(_solve_triangular)/triangular_solve | solution.py:20
  329.8 0.0 copy-done
  329.8 3.4 convolution_subtract_fusion
  333.2 2.0 fusion.6
  335.2 2.4 maximum_bitcast_fusion
  337.6 5.6 %copy.8 = f32[4096,256]{1,0:T(8,128)} copy(f32[4096,256]{0,1:T(8,128)} %maximum_bitcast_fusion) | data formatting | bytes 8388608
  343.2 0.8 copy.9
  (10 shorter events, 0.2 us)
Async XLA Ops:
  7.2 166.4 %reduce-scatter.2.cloned.1.call-start = ((), (), s32[]{:S(2)}) async-start(), calls=%async_computation.1 | async-start | bytes 20971520 | tf_op jit(solution)/shard_map/reduce_scatter | solution.py:15
  16.8 245.2 %all-gather.3.cloned.1.call-start = ((), (), s32[]{:S(2)}) async-start(), calls=%async_computation.2 | async-start | bytes 8650752 | tf_op jit(solution)/shard_map/all_gather | solution.py:19
  326.1 3.7 %copy-start = (f32[4096,256]{1,0:T(8,128)S(1)}, f32[4096,256]{1,0:T(8,128)}, u32[]{:S(2)}) copy-start(f32[4096,256]{1,0:T(8,128)} %reduce-scatter.2.cloned.1.call-done) | copy-start | bytes 12582916
Sparse Core Ops, SparseCore 0:
  17.0 156.5 reduce-scatter.1
  184.6 77.3 all-gather.2
